TPU v7x, 128 devices: a whole 4x4x4 slice. The times are simulated.
128 devices in a mesh: rep: 16 (over z_lo, x, core), shard: 8 (over z_hi, y).
Axes of the slice: x: 4, y: 4, z: 4 (z_hi: 2, z_lo: 2; z = z_hi * 2 + z_lo), core: 2. Of those that a mesh axis runs over, the one named last changes fastest.
Arguments:
- grad_embed: bfloat16 [16, 8, 4096, 768], P('rep', 'shard'), may hold values from -800 to 800
- grad_proj: bfloat16 [16, 8, 768, 768], P('rep', 'shard'), may hold values from -800 to 800
- grad_norms: bfloat16 [16, 8, 4, 768], P('rep', 'shard'), may hold values from -800 to 800
- embed_master: float32 [4096, 768], P('shard'), may hold values from -0.75 to 0.75
- embed_first: float32 [4096, 768], P('shard'), may hold values from -6 to 6
- embed_second: float32 [4096, 768], P('shard'), may hold values from 0.01 to 4
- proj_master: float32 [768, 768], P('shard'), may hold values from -0.21875 to 0.21875
- proj_first: float32 [768, 768], P('shard'), may hold values from -6 to 6
- proj_second: float32 [768, 768], P('shard'), may hold values from 0.01 to 4
- norm_master: float32 [4, 768], P(None, 'shard'), may hold values from -6 to 6
- norm_first: float32 [4, 768], P(None, 'shard'), may hold values from -6 to 6
- norm_second: float32 [4, 768], P(None, 'shard'), may hold values from 0.01 to 4
Outputs:
- embed_master_new: float32 [4096, 768], P('shard')
- embed_first_new: float32 [4096, 768], P('shard')
- embed_second_new: float32 [4096, 768], P('shard')
- embed_weights: bfloat16 [4096, 768], replicated
- proj_master_new: float32 [768, 768], P('shard')
- proj_first_new: float32 [768, 768], P('shard')
- proj_second_new: float32 [768, 768], P('shard')
- proj_weights: bfloat16 [768, 768], replicated
- norm_master_new: float32 [4, 768], P(None, 'shard')
- norm_first_new: float32 [4, 768], P(None, 'shard')
- norm_second_new: float32 [4, 768], P(None, 'shard')
- norm_weights: bfloat16 [4, 768], replicated
All inputs are finite; a program needn't handle non-finite values.
Results may differ from a plain program's by a relative error of at most 0.0004.
Values may be sent and summed in bfloat16 or wider, within the bound.
No kernel may reach another device: no remote copies, remote signals or barrier semaphores. Data moves between devices by JAX's collectives and lax.ppermute only.
A program may use at most 128 MiB of HBM per device.

v0:
```python
import jax
import jax.numpy as jnp
from jax import lax
from jax.sharding import PartitionSpec as P

beta_one = 0.9
beta_two = 0.95
adam_step = 10.0
adam_eps = 1e-08
learning_rate = 0.002
clip_rms = 1.0


def adamw(gradient, master, first, second, weight_decay):
    corr_one = 1.0 - beta_one**adam_step
    corr_two = 1.0 - beta_two**adam_step
    first_new = beta_one * first + (1.0 - beta_one) * gradient
    second_new = beta_two * second + (1.0 - beta_two) * gradient * gradient
    direction = (
        first_new / corr_one / (jnp.sqrt(second_new / corr_two) + adam_eps) + weight_decay * master
    )
    master_new = master - learning_rate * direction
    return (master_new, first_new, second_new, master_new.astype(jnp.bfloat16))


def square_sum(embed_part, proj_part, norm_part):
    return (
        jnp.sum(embed_part * embed_part)
        + jnp.sum(proj_part * proj_part)
        + jnp.sum(norm_part * norm_part)
    )


def shards(
    grad_embed,
    grad_proj,
    grad_norms,
    embed_master,
    embed_first,
    embed_second,
    proj_master,
    proj_first,
    proj_second,
    norm_master,
    norm_first,
    norm_second,
):
    embed_term = grad_embed[0, 0].astype(jnp.float32)
    proj_term = grad_proj[0, 0].astype(jnp.float32)
    norm_term = grad_norms[0, 0].astype(jnp.float32)
    embed_rows, feature_width = embed_term.shape
    proj_rows = proj_term.shape[0]
    entry_count = float(
        embed_rows * feature_width
        + proj_rows * feature_width
        + norm_term.shape[0] * norm_term.shape[1]
    )
    embed_sum, proj_sum, norm_sum = (
        lax.psum_scatter(embed_term, "shard", scatter_dimension=0, tiled=True),
        lax.psum_scatter(proj_term, "shard", scatter_dimension=0, tiled=True),
        lax.psum_scatter(norm_term, "shard", scatter_dimension=1, tiled=True),
    )
    embed_sum, proj_sum, norm_sum = lax.psum((embed_sum, proj_sum, norm_sum), "rep")
    squares = lax.psum(square_sum(embed_sum, proj_sum, norm_sum), "shard")
    rms_value = jnp.sqrt(squares / entry_count)
    clip_factor = jnp.minimum(jnp.float32(1.0), clip_rms / (rms_value + 1e-06))
    embed_out = adamw(clip_factor * embed_sum, embed_master, embed_first, embed_second, 0.01)
    proj_out = adamw(clip_factor * proj_sum, proj_master, proj_first, proj_second, 0.01)
    norm_out = adamw(clip_factor * norm_sum, norm_master, norm_first, norm_second, 0.0)
    embed_weights, proj_weights, norm_weights = (
        lax.all_gather(embed_out[3], "shard", axis=0, tiled=True),
        lax.all_gather(proj_out[3], "shard", axis=0, tiled=True),
        lax.all_gather(norm_out[3], "shard", axis=1, tiled=True),
    )
    return (
        embed_out[0],
        embed_out[1],
        embed_out[2],
        embed_weights,
        proj_out[0],
        proj_out[1],
        proj_out[2],
        proj_weights,
        norm_out[0],
        norm_out[1],
        norm_out[2],
        norm_weights,
    )


def solution(mesh):
    return jax.shard_map(
        shards,
        mesh=mesh,
        in_specs=(
            P("rep", "shard", None, None),
            P("rep", "shard", None, None),
            P("rep", "shard", None, None),
            P("shard", None),
            P("shard", None),
            P("shard", None),
            P("shard", None),
            P("shard", None),
            P("shard", None),
            P(None, "shard"),
            P(None, "shard"),
            P(None, "shard"),
        ),
        out_specs=(
            P("shard", None),
            P("shard", None),
            P("shard", None),
            P(),
            P("shard", None),
            P("shard", None),
            P("shard", None),
            P(),
            P(None, "shard"),
            P(None, "shard"),
            P(None, "shard"),
            P(),
        ),
        check_vma=False,
    )
```

profile of v0, /device:TPU:1, one launch (start us, length us, event | category | flops | bytes accessed | tf_op | source)
XLA Modules:
  0.0 624.9 jit_solution(14134784178501089757)
XLA Ops:
  7.2 0.0 reduce-scatter.8.cloned.1.call-start
  7.2 2.8 bitcast_convert_fusion.1
  10.1 0.0 reduce-scatter.8.cloned.1.call-update
  10.1 0.0 reduce-scatter.6.cloned.1.call-start
  10.1 8.3 %bitcast_convert_fusion = f32[4096,768]{1,0:T(8,128)} fusion(bf16[1,1,4096,768]{3,2,1,0:T(8,128)(2,1)} %param.12), kind=kLoop, calls=%fused_computation | loop fusion | flops 3145728 | bytes 18874368 | tf_op jit(solution)/shard_map/convert_element_type | solution.py:48
  18.5 0.0 copy-start.4
  18.5 0.0 reduce-scatter.6.cloned.1.call-update
  18.5 0.0 reduce-scatter.10.cloned.1.call-start
  18.5 0.6 copy-done.4
  19.2 0.9 copy.26
  20.1 0.0 reduce-scatter.10.cloned.1.call-update
  20.1 0.0 all-reduce.3.cloned.1.call-start
  20.2 71.8 %reduce-scatter.8.cloned.1.call-done = f32[96,768]{1,0:T(8,128)} async-done(((f32[768,768]{1,0:T(8,128)}), f32[96,768]{1,0:T(8,128)}) %reduce-scatter.8.cloned.1.call-update) | async-done | bytes 294928 | tf_op jit(solution)/shard_map/reduce_scatter | solution.py:60
  92.0 154.9 %reduce-scatter.6.cloned.1.call-done = f32[512,768]{1,0:T(8,128)} async-done(((f32[4096,768]{1,0:T(8,128)}), f32[512,768]{1,0:T(8,128)}) %reduce-scatter.6.cloned.1.call-update) | async-done | bytes 1572880 | tf_op jit(solution)/shard_map/reduce_scatter | solution.py:59
  246.9 0.0 all-reduce.3.cloned.1.call-update
  246.9 0.0 all-gather.6.cloned.1.call-start
  247.0 72.5 %reduce-scatter.10.cloned.1.call-done = f32[96,4]{1,0:T(8,128)} async-done(((f32[768,4]{1,0:T(8,128)}), f32[96,4]{1,0:T(8,128)}) %reduce-scatter.10.cloned.1.call-update) | async-done | bytes 1552
  319.5 0.9 copy.27
  320.4 29.1 %psum.30 = f32[4,96]{1,0:T(4,128)S(1)} all-reduce(f32[4,96]{1,0:T(4,128)S(1)} %copy.27), channel_id=1, replica_groups=mesh['rep'=16,'shard'=8] {'rep'}, use_global_device_ids=true, to_apply=%region_7.0 | all-reduce | flops 384 | bytes 3072 | tf_op jit(solution)/shard_map/psum | solution.py:63
  349.5 0.6 multiply_reduce_fusion.2
  350.1 95.1 %all-reduce.3.cloned.1.call-done = (f32[512,768]{1,0:T(8,128)}, f32[96,768]{1,0:T(8,128)}) async-done(((f32[512,768]{1,0:T(8,128)}, f32[96,768]{1,0:T(8,128)}), (f32[512,768]{1,0:T(8,128)}, f32[96,768]{1,0:T(8,128)})) %all-reduce.3.cloned.1.call-update) | async-done | bytes 1867792 | tf_op jit(solution)/shard_map/psum | solution.py:63
  445.2 0.0 copy-start.2
  445.2 0.0 copy-start.1
  445.2 2.6 multiply_reduce_fusion
  447.7 0.0 copy-done.2
  447.7 0.7 multiply_reduce_fusion.1
  450.3 20.7 %psum.31 = f32[]{:T(128)} all-reduce(f32[]{:T(128)S(6)} %add.69), channel_id=1, replica_groups=mesh['rep'=16,'shard'=8] {'shard'}, use_global_device_ids=true, to_apply=%region_9.0 | all-reduce | flops 1 | bytes 8 | tf_op jit(solution)/shard_map/psum | solution.py:64
  471.8 2.2 fusion.4
  474.1 0.0 all-gather.6.cloned.1.call-update
  474.1 0.0 copy-start.5
  474.1 0.0 copy-start.6
  474.1 0.0 copy-start.7
  474.1 0.0 all-gather.4.cloned.1.call-start
  474.2 0.0 copy-done.1
  474.2 0.0 copy-done
  474.2 5.1 fusion.6
  479.3 0.0 all-gather.4.cloned.1.call-update
  479.3 0.0 copy-done.5
  479.3 0.0 copy-done.6
  479.3 0.0 copy-done.7
  479.3 0.6 convert_bitcast_fusion
  479.9 14.6 %all-gather = bf16[8,96,4]{1,2,0:T(4,128)(2,1)S(1)} all-gather(bf16[1,96,4]{1,2,0:T(4,128)(2,1)S(1)} %get-tuple-element.14), channel_id=1, replica_groups=mesh['rep'=16,'shard'=8] {'shard'}, dimensions={0}, use_global_device_ids=true | all-gather | bytes 6912 | tf_op jit(solution)/shard_map/all_gather | solution.py:73
  494.6 0.7 reshape.34
  495.3 24.0 %all-gather.6.cloned.1.call-done = bf16[768,768]{1,0:T(8,128)(2,1)} async-done(((bf16[96,768]{1,0:T(8,128)(2,1)}), bf16[768,768]{1,0:T(8,128)(2,1)}) %all-gather.6.cloned.1.call-update) | async-done | bytes 1179664 | tf_op jit(solution)/shard_map/all_gather | solution.py:72
  519.3 91.7 %all-gather.4.cloned.1.call-done = bf16[4096,768]{1,0:T(8,128)(2,1)} async-done(((bf16[512,768]{1,0:T(8,128)(2,1)}), bf16[4096,768]{1,0:T(8,128)(2,1)}) %all-gather.4.cloned.1.call-update) | async-done | bytes 6291472 | tf_op jit(solution)/shard_map/all_gather | solution.py:71
  611.0 6.0 copy.32
  617.0 0.0 copy-done.3
  617.0 1.0 copy.33
  (4 shorter events, 0.0 us)
Async XLA Ops:
  7.2 84.8 %reduce-scatter.8.cloned.1.call-start = ((), (), s32[]{:S(2)}) async-start(), calls=%async_computation.4 | async-start | bytes 2654208 | tf_op jit(solution)/shard_map/reduce_scatter | solution.py:60
  10.1 236.8 %reduce-scatter.6.cloned.1.call-start = ((), (), s32[]{:S(2)}) async-start(), calls=%async_computation.3 | async-start | bytes 14155776 | tf_op jit(solution)/shard_map/reduce_scatter | solution.py:59
  18.5 0.7 copy-start.4
  18.5 301.0 %reduce-scatter.10.cloned.1.call-start = ((), (), s32[]{:S(2)}) async-start(), calls=%async_computation.7 | async-start | bytes 442368
  20.1 425.0 %all-reduce.3.cloned.1.call-start = ((), (), s32[]{:S(2)}) async-start(), calls=%async_computation.8 | async-start | bytes 3735552 | tf_op jit(solution)/shard_map/psum | solution.py:63
  246.9 272.4 %all-gather.6.cloned.1.call-start = ((), (), s32[]{:S(2)}) async-start(), calls=%async_computation.6 | async-start | bytes 1327104 | tf_op jit(solution)/shard_map/all_gather | solution.py:72
  445.2 2.6 copy-start.2
  445.2 29.0 %copy-start.1 = (f32[512,768]{1,0:T(8,128)S(1)}, f32[512,768]{1,0:T(8,128)}, u32[]{:S(2)}) copy-start(f32[512,768]{1,0:T(8,128)} %param.15) | copy-start | bytes 4718596
  447.7 26.5 %copy-start = (f32[512,768]{1,0:T(8,128)S(1)}, f32[512,768]{1,0:T(8,128)}, u32[]{:S(2)}) copy-start(f32[512,768]{1,0:T(8,128)} %get-tuple-element.12) | copy-start | bytes 4718596
  474.1 5.2 copy-start.5
  474.1 5.2 copy-start.6
  474.1 5.2 copy-start.7
  474.1 136.9 %all-gather.4.cloned.1.call-start = ((), (), s32[]{:S(2)}) async-start(), calls=%async_computation.5 | async-start | bytes 7077888 | tf_op jit(solution)/shard_map/all_gather | solution.py:71
  611.0 6.0 copy-start.3
Sparse Core Ops, SparseCore 0:
  12.4 79.5 reduce-scatter.7
  95.9 150.9 reduce-scatter.5
  251.1 68.3 reduce-scatter.9
  322.0 123.1 all-reduce.2
  474.2 45.0 all-gather.5
  522.1 88.9 all-gather.3
where the time goes:
time: 625 us
  waiting for transfers between devices  510 us (82%)
  blocking collectives  64.5 us (10%)
  other arithmetic  23 us (4%)
  between operations  16.9 us (3%)
  local copies, waits for them, and re-layouts  10.1 us (2%)
    reduce_scatter x1, waiting for transfers between devices, shards(): lax.psum_scatter(embed_term, 'shard', scatter_dimension=0, tiled=True)  155 us
    psum x1, waiting for transfers between devices, shards(): lax.psum((embed_sum, proj_sum, norm_sum), 'rep')  95.1 us
    all_gather x1, waiting for transfers between devices, shards(): lax.all_gather(embed_out[3], 'shard', axis=0, tiled=True)  91.7 us
    unnamed x7, waiting for transfers between devices  72.6 us
    reduce_scatter x1, waiting for transfers between devices, shards(): lax.psum_scatter(proj_term, 'shard', scatter_dimension=0, tiled=True)  71.8 us
    psum x1, blocking collectives, shards(): lax.psum((embed_sum, proj_sum, norm_sum), 'rep')  29.1 us
    all_gather x1, waiting for transfers between devices, shards(): lax.all_gather(proj_out[3], 'shard', axis=0, tiled=True)  24 us
    psum x1, blocking collectives, shards(): squares = lax.psum(square_sum(embed_sum, proj_sum, norm_sum), 'shard')  20.7 us
  transfers between devices with their start and end apart: 6, of which 6 were waited for; matrix products, arithmetic and copies ran while one was open for 3% of the time, Pallas kernels for 0%

commit v1 on v0

--- a/solution.py
+++ b/solution.py
@@ -9,6 +9,8 @@
 adam_eps = 1e-08
 learning_rate = 0.002
 clip_rms = 1.0
+
+ALL = ("shard", "rep")
 
 
 def adamw(gradient, master, first, second, weight_decay):
@@ -23,11 +25,10 @@
     return (master_new, first_new, second_new, master_new.astype(jnp.bfloat16))
 
 
-def square_sum(embed_part, proj_part, norm_part):
-    return (
-        jnp.sum(embed_part * embed_part)
-        + jnp.sum(proj_part * proj_part)
-        + jnp.sum(norm_part * norm_part)
+def gather_all(piece, axis):
+    count = lax.psum(1, axis)
+    return lax.all_to_all(
+        jnp.broadcast_to(piece[None], (count,) + piece.shape), axis, 0, 0, tiled=True
     )
 
 
@@ -45,33 +46,84 @@
     norm_first,
     norm_second,
 ):
-    embed_term = grad_embed[0, 0].astype(jnp.float32)
-    proj_term = grad_proj[0, 0].astype(jnp.float32)
-    norm_term = grad_norms[0, 0].astype(jnp.float32)
-    embed_rows, feature_width = embed_term.shape
-    proj_rows = proj_term.shape[0]
-    entry_count = float(
-        embed_rows * feature_width
-        + proj_rows * feature_width
-        + norm_term.shape[0] * norm_term.shape[1]
+    n_rep = lax.psum(1, "rep")
+    n_shard = lax.psum(1, "shard")
+    n_all = n_rep * n_shard
+    rep_index = lax.axis_index("rep")
+
+    embed_rows, width = grad_embed.shape[2:]
+    proj_rows = grad_proj.shape[2]
+    norm_rows, norm_cols = grad_norms.shape[2:]
+    e_rows = embed_rows // n_all
+    p_rows = proj_rows // n_all
+    n_vals = norm_rows * norm_cols // n_all
+    block_norm = norm_cols // n_shard
+    rows = e_rows + p_rows + 2
+    entry_count = float(embed_rows * width + proj_rows * width + norm_rows * norm_cols)
+
+    embed_send = grad_embed[0, 0].reshape(n_all, e_rows, width)
+    proj_send = grad_proj[0, 0].reshape(n_all, p_rows, width)
+    norm_send = (
+        grad_norms[0, 0]
+        .reshape(norm_rows, n_shard, block_norm)
+        .transpose(1, 0, 2)
+        .reshape(n_all, 1, n_vals)
     )
-    embed_sum, proj_sum, norm_sum = (
-        lax.psum_scatter(embed_term, "shard", scatter_dimension=0, tiled=True),
-        lax.psum_scatter(proj_term, "shard", scatter_dimension=0, tiled=True),
-        lax.psum_scatter(norm_term, "shard", scatter_dimension=1, tiled=True),
-    )
-    embed_sum, proj_sum, norm_sum = lax.psum((embed_sum, proj_sum, norm_sum), "rep")
-    squares = lax.psum(square_sum(embed_sum, proj_sum, norm_sum), "shard")
+    norm_send = jnp.pad(norm_send, ((0, 0), (0, 1), (0, width - n_vals)))
+    send = jnp.concatenate([embed_send, proj_send, norm_send], axis=1)
+
+    received = lax.all_to_all(send, ALL, 0, 0, tiled=True)
+    reduced = jnp.sum(received.astype(jnp.float32), axis=0)
+
+    partial = jnp.sum(reduced * reduced)
+    squares = jnp.sum(gather_all(partial.reshape(1), ALL))
     rms_value = jnp.sqrt(squares / entry_count)
     clip_factor = jnp.minimum(jnp.float32(1.0), clip_rms / (rms_value + 1e-06))
+
+    def flat_norm(x):
+        return lax.dynamic_slice(x.reshape(-1), (rep_index * n_vals,), (n_vals,))
+
+    e_piece = adamw(
+        clip_factor * reduced[:e_rows],
+        lax.dynamic_slice_in_dim(embed_master, rep_index * e_rows, e_rows),
+        lax.dynamic_slice_in_dim(embed_first, rep_index * e_rows, e_rows),
+        lax.dynamic_slice_in_dim(embed_second, rep_index * e_rows, e_rows),
+        0.01,
+    )[3]
+    p_piece = adamw(
+        clip_factor * reduced[e_rows : e_rows + p_rows],
+        lax.dynamic_slice_in_dim(proj_master, rep_index * p_rows, p_rows),
+        lax.dynamic_slice_in_dim(proj_first, rep_index * p_rows, p_rows),
+        lax.dynamic_slice_in_dim(proj_second, rep_index * p_rows, p_rows),
+        0.01,
+    )[3]
+    n_piece = adamw(
+        clip_factor * reduced[e_rows + p_rows, :n_vals],
+        flat_norm(norm_master),
+        flat_norm(norm_first),
+        flat_norm(norm_second),
+        0.0,
+    )[3]
+    n_piece = jnp.pad(n_piece.reshape(1, n_vals), ((0, 1), (0, width - n_vals)))
+    w_piece = jnp.concatenate([e_piece, p_piece, n_piece], axis=0)
+    w_all = gather_all(w_piece, ALL)
+    embed_weights = w_all[:, :e_rows].reshape(embed_rows, width)
+    proj_weights = w_all[:, e_rows : e_rows + p_rows].reshape(proj_rows, width)
+    norm_weights = (
+        w_all[:, e_rows + p_rows, :n_vals]
+        .reshape(n_shard, norm_rows, block_norm)
+        .transpose(1, 0, 2)
+        .reshape(norm_rows, norm_cols)
+    )
+
+    block = gather_all(reduced, "rep")
+    embed_sum = block[:, :e_rows].reshape(n_rep * e_rows, width)
+    proj_sum = block[:, e_rows : e_rows + p_rows].reshape(n_rep * p_rows, width)
+    norm_sum = block[:, e_rows + p_rows, :n_vals].reshape(norm_rows, block_norm)
+
     embed_out = adamw(clip_factor * embed_sum, embed_master, embed_first, embed_second, 0.01)
     proj_out = adamw(clip_factor * proj_sum, proj_master, proj_first, proj_second, 0.01)
     norm_out = adamw(clip_factor * norm_sum, norm_master, norm_first, norm_second, 0.0)
-    embed_weights, proj_weights, norm_weights = (
-        lax.all_gather(embed_out[3], "shard", axis=0, tiled=True),
-        lax.all_gather(proj_out[3], "shard", axis=0, tiled=True),
-        lax.all_gather(norm_out[3], "shard", axis=1, tiled=True),
-    )
     return (
         embed_out[0],
         embed_out[1],

time: 625 us -> 278 us (0.44)
  waiting for transfers between devices: 510 us -> 111 us
  blocking collectives: 64.5 us -> 120 us
  between operations: 16.9 us -> 1.54 us
  local copies, waits for them, and re-layouts: 10.1 us -> 21.1 us
  other arithmetic: 23 us -> 12.3 us
  starting transfers between devices: 0.24 us -> 9.8 us
    reduce_scatter x2 -> x0, waiting for transfers between devices: 227 us -> none  [the longest x1 155 us: shards(): lax.psum_scatter(embed_term, 'shard', scatter_dimension=0, tiled=True)]
    all_to_all x0 -> x2, blocking collectives: none -> 120 us  [the longest x1 103 us: shards(): received = lax.all_to_all(send, ALL, 0, 0, tiled=True)]
    all_gather x2 -> x0, waiting for transfers between devices: 116 us -> none  [the longest x1 91.7 us: shards(): lax.all_gather(embed_out[3], 'shard', axis=0, tiled=True)]
    all_to_all x0 -> x2, waiting for transfers between devices: none -> 111 us  [gather_all(): lax.all_to_all(jnp.broadcast_to(piece[None], (count,) + piece.shape), axi...]
    psum x1 -> x0, waiting for transfers between devices: 95.1 us -> none  [shards(): lax.psum((embed_sum, proj_sum, norm_sum), 'rep')]
    unnamed x7 -> x0, waiting for transfers between devices: 72.6 us -> none
    psum x2 -> x0, blocking collectives: 49.8 us -> none  [the longest x1 29.1 us: shards(): lax.psum((embed_sum, proj_sum, norm_sum), 'rep')]
    all_gather x1 -> x0, blocking collectives: 14.6 us -> none  [shards(): lax.all_gather(norm_out[3], 'shard', axis=1, tiled=True)]
  transfers between devices with their start and end apart: 6 -> 2, of which waited for: 6 -> 2; matrix products, arithmetic and copies ran while one was open for 3% -> 3% of each run, Pallas kernels for 0% -> 0%
where the time goes in v1:
time: 278 us; the launch traced here: 276 us
  blocking collectives  120 us (43%)
  waiting for transfers between devices  111 us (40%)
  local copies, waits for them, and re-layouts  21.1 us (8%)
  other arithmetic  12.3 us (4%)
  starting transfers between devices  9.8 us (4%)
    all_to_all x2, waiting for transfers between devices, gather_all(): lax.all_to_all(jnp.broadcast_to(piece[None], (count,) + piece.shape), axi...  111 us
    all_to_all x1, blocking collectives, shards(): received = lax.all_to_all(send, ALL, 0, 0, tiled=True)  103 us
    all_to_all x1, blocking collectives, gather_all(): lax.all_to_all(jnp.broadcast_to(piece[None], (count,) + piece.shape), axi...  16.4 us
    all_to_all x2, starting transfers between devices, gather_all(): lax.all_to_all(jnp.broadcast_to(piece[None], (count,) + piece.shape), axi...  9.8 us
    slice x1, local copies, waits for them, and re-layouts, shards(): embed_weights = w_all[:, :e_rows].reshape(embed_rows, width)  6.01 us
    broadcast_in_dim x3, local copies, waits for them, and re-layouts, gather_all(): jnp.broadcast_to(piece[None], (count,) + piece.shape)  5.75 us
  transfers between devices with their start and end apart: 2, of which 2 were waited for; matrix products, arithmetic and copies ran while one was open for 3% of the time, Pallas kernels for 0%

profile of v1, /device:TPU:1, one launch (start us, length us, event | category | flops | bytes accessed | tf_op | source)
XLA Modules:
  0.0 276.0 jit_solution(8230810439144185501)
XLA Ops:
  0.6 0.0 copy-start.9
  0.7 2.2 reshape_squeeze.14
  2.9 0.0 copy-done.9
  2.9 0.1 reshape_squeeze.15
  3.0 0.1 reshape.74
  3.1 3.8 %fusion.1 = bf16[128,40,768]{2,1,0:T(8,128)(2,1)S(1)} fusion(bf16[128,1,24]{2,1,0:T(2,128)(2,1)S(1)} %reshape.74, bf16[128,6,768]{2,1,0:T(8,128)(2,1)S(1)} %reshape_squeeze.14, bf16[128,32,768]{2,1,0:T(8,128)(2,1)} %bitcast.22), kind=kLoop, calls=%fused_computation.3 | loop fusion | flops 31457280 | bytes 15341568 | tf_op jit(solution)/shard_map/concatenate | solution.py:73
  6.9 103.4 %all_to_all.21 = bf16[128,40,768]{2,1,0:T(8,128)(2,1)S(1)} all-to-all(bf16[128,40,768]{2,1,0:T(8,128)(2,1)S(1)} %fusion.1), channel_id=1, replica_groups=mesh['rep'=16,'shard'=8] {'shard','rep'}, dimensions={0} | all-to-all | bytes 15728640 | tf_op jit(solution)/shard_map/all_to_all | solution.py:75
  110.3 1.1 convert_reduce_fusion
  111.4 0.6 multiply_reduce_fusion
  112.0 0.7 broadcast_in_dim.6
  112.7 16.4 %all_to_all.22 = f32[128,1,1]{2,1,0:T(1,128)S(1)} all-to-all(f32[128,1,1]{2,1,0:T(1,128)S(1)} %broadcast_in_dim.6), channel_id=1, replica_groups=mesh['rep'=16,'shard'=8] {'shard','rep'}, dimensions={0} | all-to-all | bytes 1024 | tf_op jit(solution)/shard_map/all_to_all | solution.py:30
  129.2 1.4 broadcast_in_dim.7
  130.6 0.0 copy-start.8
  130.6 0.0 copy-start.7
  130.6 0.0 copy-start.4
  130.6 0.0 copy-start.5
  130.6 4.3 %all-to-all-start.2 = ((f32[16,40,768]{2,1,0:T(8,128)}), f32[16,40,768]{2,1,0:T(8,128)S(1)}, u32[]{:S(2)}, u32[]{:S(2)}) async-start(f32[16,40,768]{2,1,0:T(8,128)} %broadcast_in_dim.7), calls=%async_computation.2 | async-start | bytes 3932160 | tf_op jit(solution)/shard_map/all_to_all | solution.py:30
  134.9 0.0 copy-done.8
  134.9 0.1 reshape.67
  135.0 0.0 copy-done.7
  135.0 0.1 reshape.68
  135.0 0.0 copy-done.6
  135.0 0.1 reshape.69
  135.1 0.7 reduce_sum.29
  136.6 0.1 convert_bitcast_fusion
  136.7 0.0 copy-done.3
  136.7 0.0 copy-done.4
  136.7 0.0 copy-done.5
  136.7 0.1 subtract_convert_fusion.1
  136.8 1.1 subtract_convert_fusion
  137.9 22.8 %all-to-all-done.2 = f32[16,40,768]{2,1,0:T(8,128)S(1)} async-done(((f32[16,40,768]{2,1,0:T(8,128)}), f32[16,40,768]{2,1,0:T(8,128)S(1)}, u32[]{:S(2)}, u32[]{:S(2)}) %all-to-all-start.2) | async-done | bytes 1966112 | tf_op jit(solution)/shard_map/all_to_all | solution.py:30
  160.7 3.7 %broadcast_in_dim.8 = bf16[128,40,768]{2,1,0:T(8,128)(2,1)} broadcast(bf16[40,768]{1,0:T(8,128)(2,1)S(1)} %fusion.12), dimensions={1,2} | broadcast | bytes 7925760 | tf_op jit(solution)/shard_map/broadcast_in_dim | solution.py:31
  164.4 5.5 %all-to-all-start.3 = ((bf16[128,40,768]{2,1,0:T(8,128)(2,1)}), bf16[128,40,768]{2,1,0:T(8,128)(2,1)}, u32[]{:S(2)}, u32[]{:S(2)}) async-start(bf16[128,40,768]{2,1,0:T(8,128)(2,1)} %broadcast_in_dim.8), calls=%async_computation.3 | async-start | bytes 15728640 | tf_op jit(solution)/shard_map/all_to_all | solution.py:30
  170.0 0.1 mul.362
  170.1 0.6 multiply_subtract_fusion.2
  170.7 1.0 multiply_subtract_fusion.1
  171.8 0.2 slice_multiply_fusion
  171.9 0.5 copy-done.2
  172.4 0.8 copy-done
  173.3 0.5 copy-done.1
  173.8 3.0 %multiply_subtract_fusion = (f32[512,768]{1,0:T(8,128)}, f32[512,768]{1,0:T(8,128)}, f32[512,768]{1,0:T(8,128)}) fusion(f32[512,768]{1,0:T(8,128)S(1)} %copy-done, f32[16,32,768]{2,1,0:T(8,128)S(1)} %slice_multiply_fusion, f32[512,768]{1,0:T(8,128)S(1)} %copy-done.1, f32[512,768]{1,0:T(8,128)S(1)} %copy-done.2), kind=kLoop, calls=%fused_computation.9 | loop fusion | flops 5898240 | bytes 11010048 | tf_op jit(solution)/shard_map/sub | solution.py:24
  176.7 88.6 %all-to-all-done.3 = bf16[128,40,768]{2,1,0:T(8,128)(2,1)} async-done(((bf16[128,40,768]{2,1,0:T(8,128)(2,1)}), bf16[128,40,768]{2,1,0:T(8,128)(2,1)}, u32[]{:S(2)}, u32[]{:S(2)}) %all-to-all-start.3) | async-done | bytes 7864352 | tf_op jit(solution)/shard_map/all_to_all | solution.py:30
  265.3 1.5 slice.42
  266.8 1.2 reshape.72
  268.1 1.2 slice_reduce_fusion
  269.2 0.1 reshape_squeeze.16
  269.3 0.7 reshape.73
  270.0 6.0 %slice.40 = bf16[128,32,768]{2,1,0:T(8,128)(2,1)} slice(bf16[128,40,768]{2,1,0:T(8,128)(2,1)} %all-to-all-done.3), slice={[0:128], [0:32], [0:768]} | slice | bytes 12582912 | tf_op jit(solution)/shard_map/slice | solution.py:110
  (11 shorter events, 0.1 us)
Async XLA Ops:
  0.6 2.3 copy-start.9
  130.6 4.3 %copy-start.8 = (f32[4,96]{1,0:T(4,128)S(1)}, f32[4,96]{1,0:T(4,128)}, u32[]{:S(2)}) copy-start(f32[4,96]{1,0:T(4,128)} %param.21) | copy-start | bytes 4612
  130.6 4.4 %copy-start.7 = (f32[4,96]{1,0:T(4,128)S(1)}, f32[4,96]{1,0:T(4,128)}, u32[]{:S(2)}) copy-start(f32[4,96]{1,0:T(4,128)} %param.22) | copy-start | bytes 4612
  130.6 4.5 %copy-start.6 = (f32[4,96]{1,0:T(4,128)S(1)}, f32[4,96]{1,0:T(4,128)}, u32[]{:S(2)}) copy-start(f32[4,96]{1,0:T(4,128)} %param.23) | copy-start | bytes 4612
  130.6 6.1 %copy-start.3 = (f32[96,768]{1,0:T(8,128)S(1)}, f32[96,768]{1,0:T(8,128)}, u32[]{:S(2)}) copy-start(f32[96,768]{1,0:T(8,128)} %param.20) | copy-start | bytes 884740
  130.6 6.1 %copy-start.4 = (f32[96,768]{1,0:T(8,128)S(1)}, f32[96,768]{1,0:T(8,128)}, u32[]{:S(2)}) copy-start(f32[96,768]{1,0:T(8,128)} %param.19) | copy-start | bytes 884740
  130.6 6.1 %copy-start.5 = (f32[96,768]{1,0:T(8,128)S(1)}, f32[96,768]{1,0:T(8,128)}, u32[]{:S(2)}) copy-start(f32[96,768]{1,0:T(8,128)} %param.18) | copy-start | bytes 884740
  130.6 30.1 %all-to-all-start.2 = ((f32[16,40,768]{2,1,0:T(8,128)}), f32[16,40,768]{2,1,0:T(8,128)S(1)}, u32[]{:S(2)}, u32[]{:S(2)}) async-start(f32[16,40,768]{2,1,0:T(8,128)} %broadcast_in_dim.7), calls=%async_computation.2 | async-start | bytes 3932160 | tf_op jit(solution)/shard_map/all_to_all | solution.py:30
  164.4 100.9 %all-to-all-start.3 = ((bf16[128,40,768]{2,1,0:T(8,128)(2,1)}), bf16[128,40,768]{2,1,0:T(8,128)(2,1)}, u32[]{:S(2)}, u32[]{:S(2)}) async-start(bf16[128,40,768]{2,1,0:T(8,128)(2,1)} %broadcast_in_dim.8), calls=%async_computation.3 | async-start | bytes 15728640 | tf_op jit(solution)/shard_map/all_to_all | solution.py:30
  170.7 1.7 copy-start.2
  171.8 1.5 copy-start
  171.8 2.0 copy-start.1

commit v2 on v1

--- a/solution.py
+++ b/solution.py
@@ -116,7 +116,7 @@
         .reshape(norm_rows, norm_cols)
     )
 
-    block = gather_all(reduced, "rep")
+    block = lax.all_gather(reduced, "rep", axis=0)
     embed_sum = block[:, :e_rows].reshape(n_rep * e_rows, width)
     proj_sum = block[:, e_rows : e_rows + p_rows].reshape(n_rep * p_rows, width)
     norm_sum = block[:, e_rows + p_rows, :n_vals].reshape(norm_rows, block_norm)

time: 278 us -> 304 us (1.094)
  blocking collectives: 120 us -> 0 us
  waiting for transfers between devices: 111 us -> 215 us
  starting transfers between devices: 9.8 us -> 27.9 us
  between operations: 1.54 us -> 14.9 us
  other arithmetic: 12.3 us -> 23.5 us
    all_to_all x2 -> x0, blocking collectives: 120 us -> none  [the longest x1 103 us: shards(): received = lax.all_to_all(send, ALL, 0, 0, tiled=True)]
    all_gather x0 -> x1, waiting for transfers between devices: none -> 110 us  [shards(): block = lax.all_gather(reduced, 'rep', axis=0)]
    all_to_all x2, waiting for transfers between devices: 111 us -> 9.58 us  [gather_all(): lax.all_to_all(jnp.broadcast_to(piece[None], (count,) + piece.shape), axi...]
    all_to_all x0 -> x1, waiting for transfers between devices: none -> 95.3 us  [shards(): received = lax.all_to_all(send, ALL, 0, 0, tiled=True)]
    all_to_all x0 -> x1, starting transfers between devices: none -> 11.9 us  [shards(): received = lax.all_to_all(send, ALL, 0, 0, tiled=True)]
    all_to_all x2, starting transfers between devices: 9.8 us -> 15.9 us  [gather_all(): lax.all_to_all(jnp.broadcast_to(piece[None], (count,) + piece.shape), axi...]
    reduce_sum x1, other arithmetic: 1.09 us -> 4.34 us  [shards(): reduced = jnp.sum(received.astype(jnp.float32), axis=0)]
  transfers between devices with their start and end apart: 2 -> 4, of which waited for: 2 -> 3; matrix products, arithmetic and copies ran while one was open for 3% -> 4% of each run, Pallas kernels for 0% -> 0%
where the time goes in v2:
time: 304 us
  waiting for transfers between devices  215 us (71%)
  starting transfers between devices  27.9 us (9%)
  other arithmetic  23.5 us (8%)
  local copies, waits for them, and re-layouts  22.1 us (7%)
  between operations  14.9 us (5%)
    all_gather x1, waiting for transfers between devices, shards(): block = lax.all_gather(reduced, 'rep', axis=0)  110 us
    all_to_all x1, waiting for transfers between devices, shards(): received = lax.all_to_all(send, ALL, 0, 0, tiled=True)  95.3 us
    all_to_all x2, starting transfers between devices, gather_all(): lax.all_to_all(jnp.broadcast_to(piece[None], (count,) + piece.shape), axi...  15.9 us
    all_to_all x1, starting transfers between devices, shards(): received = lax.all_to_all(send, ALL, 0, 0, tiled=True)  11.9 us
    all_to_all x2, waiting for transfers between devices, gather_all(): lax.all_to_all(jnp.broadcast_to(piece[None], (count,) + piece.shape), axi...  9.58 us
    sub x3, other arithmetic, adamw(): master_new = master - learning_rate * direction  6.54 us
    concatenate x1, other arithmetic, shards(): send = jnp.concatenate([embed_send, proj_send, norm_send], axis=1)  6.41 us
  transfers between devices with their start and end apart: 4, of which 3 were waited for; matrix products, arithmetic and copies ran while one was open for 4% of the time, Pallas kernels for 0%

profile of v2, /device:TPU:1, one launch (start us, length us, event | category | flops | bytes accessed | tf_op | source)
XLA Modules:
  0.0 303.5 jit_solution(8518624998814067983)
XLA Ops:
  7.2 0.0 copy-start.8
  7.2 2.2 reshape_squeeze.14
  9.4 0.0 copy-done.8
  9.4 0.1 reshape_squeeze.15
  9.5 0.1 reshape.74
  9.6 6.4 %fusion.1 = bf16[128,40,768]{2,1,0:T(8,128)(2,1)} fusion(bf16[128,1,24]{2,1,0:T(2,128)(2,1)S(1)} %reshape.74, bf16[128,6,768]{2,1,0:T(8,128)(2,1)S(1)} %reshape_squeeze.14, bf16[128,32,768]{2,1,0:T(8,128)(2,1)} %bitcast.23), kind=kLoop, calls=%fused_computation.3 | loop fusion | flops 31457280 | bytes 15341568 | tf_op jit(solution)/shard_map/concatenate | solution.py:73
  16.0 11.9 %all-to-all-start = ((bf16[128,40,768]{2,1,0:T(8,128)(2,1)}), bf16[128,40,768]{2,1,0:T(8,128)(2,1)}, u32[]{:S(2)}, u32[]{:S(2)}) async-start(bf16[128,40,768]{2,1,0:T(8,128)(2,1)} %fusion.1), calls=%async_computation | async-start | bytes 15728640 | tf_op jit(solution)/shard_map/all_to_all | solution.py:75
  27.9 0.0 copy-start.7
  27.9 0.0 copy-start.6
  28.0 0.0 copy-start.5
  28.0 0.0 copy-start.2
  28.0 95.3 %all-to-all-done = bf16[128,40,768]{2,1,0:T(8,128)(2,1)} async-done(((bf16[128,40,768]{2,1,0:T(8,128)(2,1)}), bf16[128,40,768]{2,1,0:T(8,128)(2,1)}, u32[]{:S(2)}, u32[]{:S(2)}) %all-to-all-start) | async-done | bytes 7864352 | tf_op jit(solution)/shard_map/all_to_all | solution.py:75
  123.3 4.3 %convert_reduce_fusion = f32[40,768]{1,0:T(8,128)S(1)} fusion(bf16[128,40,768]{2,1,0:T(8,128)(2,1)} %all-to-all-done), kind=kLoop, calls=%fused_computation.1 | loop fusion | flops 7833600 | bytes 7987200 | tf_op jit(solution)/shard_map/reduce_sum | solution.py:76
  127.7 0.6 multiply_reduce_fusion
  128.3 1.3 broadcast_in_dim.4
  129.6 10.7 %all-to-all-start.1 = ((f32[128,1,1]{2,1,0:T(1,128)}), f32[128,1,1]{2,1,0:T(1,128)S(1)}, u32[]{:S(2)}, u32[]{:S(2)}) async-start(f32[128,1,1]{2,1,0:T(1,128)} %broadcast_in_dim.4), calls=%async_computation.1 | async-start | bytes 131072 | tf_op jit(solution)/shard_map/all_to_all | solution.py:30
  140.4 0.1 reshape.66
  140.5 0.1 reshape.67
  140.5 0.0 copy-done.5
  140.5 0.1 reshape.68
  140.6 9.6 %all-to-all-done.1 = f32[128,1,1]{2,1,0:T(1,128)S(1)} async-done(((f32[128,1,1]{2,1,0:T(1,128)}), f32[128,1,1]{2,1,0:T(1,128)S(1)}, u32[]{:S(2)}, u32[]{:S(2)}) %all-to-all-start.1) | async-done | bytes 544 | tf_op jit(solution)/shard_map/all_to_all | solution.py:30
  150.2 0.7 reduce_sum.29
  151.7 0.0 copy-done.2
  151.7 1.0 subtract_convert_fusion
  152.7 0.9 subtract_convert_fusion.1
  153.6 0.1 convert_bitcast_fusion
  153.7 3.7 %broadcast_in_dim.5 = bf16[128,40,768]{2,1,0:T(8,128)(2,1)} broadcast(bf16[40,768]{1,0:T(8,128)(2,1)S(1)} %fusion.12), dimensions={1,2} | broadcast | bytes 7925760 | tf_op jit(solution)/shard_map/broadcast_in_dim | solution.py:31
  157.4 5.2 %all-to-all-start.2 = ((bf16[128,40,768]{2,1,0:T(8,128)(2,1)}), bf16[128,40,768]{2,1,0:T(8,128)(2,1)}, u32[]{:S(2)}, u32[]{:S(2)}) async-start(bf16[128,40,768]{2,1,0:T(8,128)(2,1)} %broadcast_in_dim.5), calls=%async_computation.2 | async-start | bytes 15728640 | tf_op jit(solution)/shard_map/all_to_all | solution.py:30
  162.6 0.0 all-gather.3.cloned.1.call-start
  162.6 0.7 all-gather.3.cloned.1.call-update
  163.3 109.6 %all-gather.3.cloned.1.call-done = f32[640,768]{1,0:T(8,128)} async-done(((f32[40,768]{1,0:T(8,128)}), f32[640,768]{1,0:T(8,128)}) %all-gather.3.cloned.1.call-update) | async-done | bytes 1966096 | tf_op jit(solution)/shard_map/all_gather | solution.py:119
  272.9 1.8 slice_multiply_fusion.1
  274.7 1.9 mul.346
  276.6 0.9 fusion.19
  277.4 0.1 mul.362
  277.5 1.3 multiply_subtract_fusion.2
  278.8 2.3 multiply_subtract_fusion.1
  281.1 0.2 slice_multiply_fusion
  281.3 1.2 copy-done.3
  282.5 0.5 copy-done.4
  283.0 3.0 multiply_subtract_fusion
  285.9 0.0 all-to-all-done.2
  285.9 1.5 slice.42
  287.5 1.2 reshape.71
  288.7 1.2 slice_reduce_fusion
  289.9 0.1 reshape_squeeze.16
  290.0 0.7 reshape.72
  290.7 6.0 %slice.40 = bf16[128,32,768]{2,1,0:T(8,128)(2,1)} slice(bf16[128,40,768]{2,1,0:T(8,128)(2,1)} %all-to-all-done.2), slice={[0:128], [0:32], [0:768]} | slice | bytes 12582912 | tf_op jit(solution)/shard_map/slice | solution.py:110
  (11 shorter events, 0.0 us)
Async XLA Ops:
  7.2 2.3 copy-start.8
  16.0 107.3 %all-to-all-start = ((bf16[128,40,768]{2,1,0:T(8,128)(2,1)}), bf16[128,40,768]{2,1,0:T(8,128)(2,1)}, u32[]{:S(2)}, u32[]{:S(2)}) async-start(bf16[128,40,768]{2,1,0:T(8,128)(2,1)} %fusion.1), calls=%async_computation | async-start | bytes 15728640 | tf_op jit(solution)/shard_map/all_to_all | solution.py:75
  27.9 112.4 %copy-start.7 = (f32[4,96]{1,0:T(4,128)S(1)}, f32[4,96]{1,0:T(4,128)}, u32[]{:S(2)}) copy-start(f32[4,96]{1,0:T(4,128)} %param.21) | copy-start | bytes 4612
  27.9 112.5 %copy-start.6 = (f32[4,96]{1,0:T(4,128)S(1)}, f32[4,96]{1,0:T(4,128)}, u32[]{:S(2)}) copy-start(f32[4,96]{1,0:T(4,128)} %param.22) | copy-start | bytes 4612
  28.0 112.6 %copy-start.5 = (f32[4,96]{1,0:T(4,128)S(1)}, f32[4,96]{1,0:T(4,128)}, u32[]{:S(2)}) copy-start(f32[4,96]{1,0:T(4,128)} %param.23) | copy-start | bytes 4612
  28.0 123.7 %copy-start.2 = (f32[512,768]{1,0:T(8,128)S(1)}, f32[512,768]{1,0:T(8,128)}, u32[]{:S(2)}) copy-start(f32[512,768]{1,0:T(8,128)} %param.15) | copy-start | bytes 4718596
  127.7 29.7 %copy-start.1 = (f32[40,768]{1,0:T(8,128)}, f32[40,768]{1,0:T(8,128)S(1)}, u32[]{:S(2)}) copy-start(f32[40,768]{1,0:T(8,128)S(1)} %convert_reduce_fusion) | copy-start | bytes 368644
  129.6 20.6 %all-to-all-start.1 = ((f32[128,1,1]{2,1,0:T(1,128)}), f32[128,1,1]{2,1,0:T(1,128)S(1)}, u32[]{:S(2)}, u32[]{:S(2)}) async-start(f32[128,1,1]{2,1,0:T(1,128)} %broadcast_in_dim.4), calls=%async_computation.1 | async-start | bytes 131072 | tf_op jit(solution)/shard_map/all_to_all | solution.py:30
  157.4 128.6 %all-to-all-start.2 = ((bf16[128,40,768]{2,1,0:T(8,128)(2,1)}), bf16[128,40,768]{2,1,0:T(8,128)(2,1)}, u32[]{:S(2)}, u32[]{:S(2)}) async-start(bf16[128,40,768]{2,1,0:T(8,128)(2,1)} %broadcast_in_dim.5), calls=%async_computation.2 | async-start | bytes 15728640 | tf_op jit(solution)/shard_map/all_to_all | solution.py:30
  162.6 110.3 %all-gather.3.cloned.1.call-start = ((), (), s32[]{:S(2)}) async-start(), calls=%async_computation.3 | async-start | bytes 2088960 | tf_op jit(solution)/shard_map/all_gather | solution.py:119
  274.7 6.4 %copy-start = (f32[640,768]{1,0:T(8,128)S(1)}, f32[640,768]{1,0:T(8,128)}, u32[]{:S(2)}) copy-start(f32[640,768]{1,0:T(8,128)} %all-gather.3.cloned.1.call-done) | copy-start | bytes 5898244
  281.1 1.4 copy-start.3
  281.1 1.9 copy-start.4
Sparse Core Ops, SparseCore 0:
  165.7 107.1 all-gather.2

commit v3 on v2

--- a/solution.py
+++ b/solution.py
@@ -10,7 +10,8 @@
 learning_rate = 0.002
 clip_rms = 1.0
 
-ALL = ("shard", "rep")
+ALL = ("shard", "rep_hi", "core")
+HALF = ("shard", "rep_hi")
 
 
 def adamw(gradient, master, first, second, weight_decay):
@@ -46,10 +47,11 @@
     norm_first,
     norm_second,
 ):
-    n_rep = lax.psum(1, "rep")
+    n_rep = lax.psum(1, ("rep_hi", "core"))
     n_shard = lax.psum(1, "shard")
     n_all = n_rep * n_shard
-    rep_index = lax.axis_index("rep")
+    rep_index = lax.axis_index(("rep_hi", "core"))
+    core = lax.axis_index("core")
 
     embed_rows, width = grad_embed.shape[2:]
     proj_rows = grad_proj.shape[2]
@@ -106,7 +108,11 @@
     )[3]
     n_piece = jnp.pad(n_piece.reshape(1, n_vals), ((0, 1), (0, width - n_vals)))
     w_piece = jnp.concatenate([e_piece, p_piece, n_piece], axis=0)
-    w_all = gather_all(w_piece, ALL)
+    w_mine = gather_all(w_piece, HALF)
+    w_other = lax.ppermute(w_mine, "core", [(0, 1), (1, 0)])
+    w_all = jnp.stack(
+        [jnp.where(core == 0, w_mine, w_other), jnp.where(core == 0, w_other, w_mine)], axis=1
+    ).reshape((n_all,) + w_piece.shape)
     embed_weights = w_all[:, :e_rows].reshape(embed_rows, width)
     proj_weights = w_all[:, e_rows : e_rows + p_rows].reshape(proj_rows, width)
     norm_weights = (
@@ -116,7 +122,7 @@
         .reshape(norm_rows, norm_cols)
     )
 
-    block = lax.all_gather(reduced, "rep", axis=0)
+    block = gather_all(reduced, ("rep_hi", "core"))
     embed_sum = block[:, :e_rows].reshape(n_rep * e_rows, width)
     proj_sum = block[:, e_rows : e_rows + p_rows].reshape(n_rep * p_rows, width)
     norm_sum = block[:, e_rows + p_rows, :n_vals].reshape(norm_rows, block_norm)
@@ -141,13 +147,18 @@
 
 
 def solution(mesh):
+    n_rep, n_shard = mesh.devices.shape
+    fine = jax.sharding.Mesh(
+        mesh.devices.reshape(n_rep // 2, 2, n_shard), ("rep_hi", "core", "shard")
+    )
+    rep = ("rep_hi", "core")
     return jax.shard_map(
         shards,
-        mesh=mesh,
+        mesh=fine,
         in_specs=(
-            P("rep", "shard", None, None),
-            P("rep", "shard", None, None),
-            P("rep", "shard", None, None),
+            P(rep, "shard", None, None),
+            P(rep, "shard", None, None),
+            P(rep, "shard", None, None),
             P("shard", None),
             P("shard", None),
             P("shard", None),

time: 304 us -> 263 us (0.87)
  waiting for transfers between devices: 215 us -> 131 us
  blocking collectives: 0 us -> 53.7 us
  between operations: 14.9 us -> 1.56 us
  other arithmetic: 23.5 us -> 29 us
  local copies, waits for them, and re-layouts: 22.1 us -> 19 us
    all_gather x1 -> x0, waiting for transfers between devices: 110 us -> none  [shards(): block = lax.all_gather(reduced, 'rep', axis=0)]
    all_to_all x0 -> x1, blocking collectives: none -> 53.7 us  [gather_all(): lax.all_to_all(jnp.broadcast_to(piece[None], (count,) + piece.shape), axi...]
    all_to_all x2, waiting for transfers between devices: 9.58 us -> 35.3 us  [gather_all(): lax.all_to_all(jnp.broadcast_to(piece[None], (count,) + piece.shape), axi...]
    another operation x0 -> x2, other arithmetic: none -> 7.34 us  [shards(): jnp.stack([jnp.where(core == 0, w_mine, w_other), jnp.where(core == 0, w_...]
    another operation x0 -> x1, local copies, waits for them, and re-layouts: none -> 3.83 us  [shards(): jnp.stack([jnp.where(core == 0, w_mine, w_other), jnp.where(core == 0, w_...]
where the time goes in v3:
time: 263 us; the launch traced here: 262 us
  waiting for transfers between devices  131 us (50%)
  blocking collectives  53.7 us (20%)
  other arithmetic  29 us (11%)
  starting transfers between devices  27.9 us (11%)
  local copies, waits for them, and re-layouts  19 us (7%)
    all_to_all x1, waiting for transfers between devices, shards(): received = lax.all_to_all(send, ALL, 0, 0, tiled=True)  95.3 us
    all_to_all x1, blocking collectives, gather_all(): lax.all_to_all(jnp.broadcast_to(piece[None], (count,) + piece.shape), axi...  53.7 us
    all_to_all x2, waiting for transfers between devices, gather_all(): lax.all_to_all(jnp.broadcast_to(piece[None], (count,) + piece.shape), axi...  35.3 us
    all_to_all x2, starting transfers between devices, gather_all(): lax.all_to_all(jnp.broadcast_to(piece[None], (count,) + piece.shape), axi...  14.3 us
    all_to_all x1, starting transfers between devices, shards(): received = lax.all_to_all(send, ALL, 0, 0, tiled=True)  11.9 us
    another operation x2, other arithmetic, shards(): jnp.stack([jnp.where(core == 0, w_mine, w_other), jnp.where(core == 0, w_...  7.34 us
    sub x3, other arithmetic, adamw(): master_new = master - learning_rate * direction  6.53 us
    concatenate x1, other arithmetic, shards(): send = jnp.concatenate([embed_send, proj_send, norm_send], axis=1)  6.4 us
  transfers between devices with their start and end apart: 4, of which 3 were waited for; matrix products, arithmetic and copies ran while one was open for 4% of the time, Pallas kernels for 0%

profile of v3, /device:TPU:1, one launch (start us, length us, event | category | flops | bytes accessed | tf_op | source)
XLA Modules:
  0.0 261.7 jit_solution(4125089683993481099)
XLA Ops:
  0.7 2.2 reshape_squeeze.14
  2.9 0.0 copy-done.6
  2.9 0.1 reshape_squeeze.15
  3.0 0.1 reshape.78
  3.1 6.4 %fusion.1 = bf16[128,40,768]{2,1,0:T(8,128)(2,1)} fusion(bf16[128,1,24]{2,1,0:T(2,128)(2,1)S(1)} %reshape.78, bf16[128,6,768]{2,1,0:T(8,128)(2,1)S(1)} %reshape_squeeze.14, bf16[128,32,768]{2,1,0:T(8,128)(2,1)} %bitcast.30), kind=kLoop, calls=%fused_computation.3 | loop fusion | flops 31457280 | bytes 15341568 | tf_op jit(solution)/shard_map/concatenate | solution.py:75
  9.5 11.9 %all-to-all-start = ((bf16[128,40,768]{2,1,0:T(8,128)(2,1)}), bf16[128,40,768]{2,1,0:T(8,128)(2,1)}, u32[]{:S(2)}, u32[]{:S(2)}) async-start(bf16[128,40,768]{2,1,0:T(8,128)(2,1)} %fusion.1), calls=%async_computation | async-start | bytes 15728640 | tf_op jit(solution)/shard_map/all_to_all | solution.py:77
  21.4 0.0 copy-start.5
  21.4 0.0 copy-start.4
  21.4 0.0 copy-start.3
  21.4 0.0 copy-start
  21.5 95.3 %all-to-all-done = bf16[128,40,768]{2,1,0:T(8,128)(2,1)} async-done(((bf16[128,40,768]{2,1,0:T(8,128)(2,1)}), bf16[128,40,768]{2,1,0:T(8,128)(2,1)}, u32[]{:S(2)}, u32[]{:S(2)}) %all-to-all-start) | async-done | bytes 7864352 | tf_op jit(solution)/shard_map/all_to_all | solution.py:77
  116.8 4.3 %convert_reduce_fusion = f32[40,768]{1,0:T(8,128)S(1)} fusion(bf16[128,40,768]{2,1,0:T(8,128)(2,1)} %all-to-all-done), kind=kLoop, calls=%fused_computation.1 | loop fusion | flops 7833600 | bytes 7987200 | tf_op jit(solution)/shard_map/reduce_sum | solution.py:78
  121.1 0.6 multiply_reduce_fusion
  121.8 1.3 broadcast_in_dim.6
  123.1 10.7 %all-to-all-start.1 = ((f32[128,1,1]{2,1,0:T(1,128)}), f32[128,1,1]{2,1,0:T(1,128)S(1)}, u32[]{:S(2)}, u32[]{:S(2)}) async-start(f32[128,1,1]{2,1,0:T(1,128)} %broadcast_in_dim.6), calls=%async_computation.1 | async-start | bytes 131072 | tf_op jit(solution)/shard_map/all_to_all | solution.py:31
  133.8 0.1 reshape.70
  133.9 0.1 reshape.71
  134.0 0.1 reshape.72
  134.1 9.6 %all-to-all-done.1 = f32[128,1,1]{2,1,0:T(1,128)S(1)} async-done(((f32[128,1,1]{2,1,0:T(1,128)}), f32[128,1,1]{2,1,0:T(1,128)S(1)}, u32[]{:S(2)}, u32[]{:S(2)}) %all-to-all-start.1) | async-done | bytes 544 | tf_op jit(solution)/shard_map/all_to_all | solution.py:31
  143.7 0.7 reduce_sum.29
  145.1 1.0 subtract_convert_fusion
  146.2 0.9 subtract_convert_fusion.1
  147.1 0.1 convert_bitcast_fusion
  147.2 0.3 broadcast_in_dim.8
  147.5 53.7 %all_to_all.21 = bf16[64,40,768]{2,1,0:T(8,128)(2,1)} all-to-all(bf16[64,40,768]{2,1,0:T(8,128)(2,1)S(1)} %broadcast_in_dim.8), channel_id=1, replica_groups=mesh['rep_hi'=8,'core'=2,'shard'=8] {'shard','rep_hi'}, dimensions={0} | all-to-all | bytes 7864320 | tf_op jit(solution)/shard_map/all_to_all | solution.py:31
  201.1 1.7 collective-permute-start
  202.8 1.4 broadcast_in_dim.7
  204.2 3.6 %all-to-all-start.2 = ((f32[16,40,768]{2,1,0:T(8,128)}), f32[16,40,768]{2,1,0:T(8,128)S(1)}, u32[]{:S(2)}, u32[]{:S(2)}) async-start(f32[16,40,768]{2,1,0:T(8,128)} %broadcast_in_dim.7), calls=%async_computation.2 | async-start | bytes 3932160 | tf_op jit(solution)/shard_map/all_to_all | solution.py:31
  207.9 25.7 %all-to-all-done.2 = f32[16,40,768]{2,1,0:T(8,128)S(1)} async-done(((f32[16,40,768]{2,1,0:T(8,128)}), f32[16,40,768]{2,1,0:T(8,128)S(1)}, u32[]{:S(2)}, u32[]{:S(2)}) %all-to-all-start.2) | async-done | bytes 1966112 | tf_op jit(solution)/shard_map/all_to_all | solution.py:31
  233.6 0.8 slice_multiply_fusion.1
  234.3 1.8 mul.350
  236.1 0.1 mul.366
  236.2 1.3 multiply_subtract_fusion.2
  237.5 2.3 multiply_subtract_fusion.1
  239.8 0.2 slice_multiply_fusion
  239.9 1.2 copy-done.1
  241.2 0.5 copy-done.2
  241.7 3.0 %multiply_subtract_fusion = (f32[512,768]{1,0:T(8,128)}, f32[512,768]{1,0:T(8,128)}, f32[512,768]{1,0:T(8,128)}) fusion(f32[512,768]{1,0:T(8,128)S(1)} %copy-done, f32[16,32,768]{2,1,0:T(8,128)S(1)} %slice_multiply_fusion, f32[512,768]{1,0:T(8,128)S(1)} %copy-done.1, f32[512,768]{1,0:T(8,128)S(1)} %copy-done.2), kind=kLoop, calls=%fused_computation.12 | loop fusion | flops 5898240 | bytes 11010048 | tf_op jit(solution)/shard_map/sub | solution.py:25
  244.6 0.0 collective-permute-done
  244.6 3.6 %select_bitcast_fusion.1 = (bf16[64,1,40,768]{3,2,0,1:T(8,128)(2,1)S(1)}, bf16[64,1,40,768]{3,2,0,1:T(8,128)(2,1)S(1)}) fusion(bf16[64,40,768]{2,1,0:T(8,128)(2,1)} %all_to_all.21, bf16[64,40,768]{2,1,0:T(8,128)(2,1)} %collective-permute-done, pred[]{:T(512)S(6)} %eq.4), kind=kLoop, calls=%fused_computation.6 | loop fusion | flops 3932160 | bytes 15728641 | tf_op jit(solution)/shard_map/stack | solution.py:113
  248.2 3.7 %pad_maximum_fusion = bf16[64,2,40,768]{3,2,0,1:T(8,128)(2,1)} fusion(bf16[64,1,40,768]{3,2,0,1:T(8,128)(2,1)S(1)} %get-tuple-element.22, bf16[64,1,40,768]{3,2,0,1:T(8,128)(2,1)S(1)} %get-tuple-element.21), kind=kLoop, calls=%fused_computation.4 | loop fusion | flops 3932160 | bytes 15728640 | tf_op jit(solution)/shard_map/stack | solution.py:113
  252.0 3.8 %copy.48 = bf16[64,2,40,768]{3,2,1,0:T(8,128)(2,1)S(1)} copy(bf16[64,2,40,768]{3,2,0,1:T(8,128)(2,1)} %pad_maximum_fusion) | data formatting | bytes 15728640 | tf_op jit(solution)/shard_map/stack | solution.py:113
  255.8 3.6 %slice.40 = bf16[128,32,768]{2,1,0:T(8,128)(2,1)} slice(bf16[128,40,768]{2,1,0:T(8,128)(2,1)S(1)} %bitcast.26), slice={[0:128], [0:32], [0:768]} | slice | bytes 12582912 | tf_op jit(solution)/shard_map/slice | solution.py:116
  259.4 0.1 slice.42
  259.5 0.2 slice_reduce_fusion
  259.7 1.2 reshape.76
  261.0 0.1 reshape_squeeze.16
  261.1 0.7 reshape.77
  (11 shorter events, 0.1 us)
Async XLA Ops:
  0.6 2.3 copy-start.6
  9.5 107.3 %all-to-all-start = ((bf16[128,40,768]{2,1,0:T(8,128)(2,1)}), bf16[128,40,768]{2,1,0:T(8,128)(2,1)}, u32[]{:S(2)}, u32[]{:S(2)}) async-start(bf16[128,40,768]{2,1,0:T(8,128)(2,1)} %fusion.1), calls=%async_computation | async-start | bytes 15728640 | tf_op jit(solution)/shard_map/all_to_all | solution.py:77
  21.4 112.4 %copy-start.5 = (f32[4,96]{1,0:T(4,128)S(1)}, f32[4,96]{1,0:T(4,128)}, u32[]{:S(2)}) copy-start(f32[4,96]{1,0:T(4,128)} %param.21) | copy-start | bytes 4612
  21.4 112.5 %copy-start.4 = (f32[4,96]{1,0:T(4,128)S(1)}, f32[4,96]{1,0:T(4,128)}, u32[]{:S(2)}) copy-start(f32[4,96]{1,0:T(4,128)} %param.22) | copy-start | bytes 4612
  21.4 112.6 %copy-start.3 = (f32[4,96]{1,0:T(4,128)S(1)}, f32[4,96]{1,0:T(4,128)}, u32[]{:S(2)}) copy-start(f32[4,96]{1,0:T(4,128)} %param.23) | copy-start | bytes 4612
  21.4 123.7 %copy-start = (f32[512,768]{1,0:T(8,128)S(1)}, f32[512,768]{1,0:T(8,128)}, u32[]{:S(2)}) copy-start(f32[512,768]{1,0:T(8,128)} %param.15) | copy-start | bytes 4718596
  123.1 20.6 %all-to-all-start.1 = ((f32[128,1,1]{2,1,0:T(1,128)}), f32[128,1,1]{2,1,0:T(1,128)S(1)}, u32[]{:S(2)}, u32[]{:S(2)}) async-start(f32[128,1,1]{2,1,0:T(1,128)} %broadcast_in_dim.6), calls=%async_computation.1 | async-start | bytes 131072 | tf_op jit(solution)/shard_map/all_to_all | solution.py:31
  201.1 43.5 %collective-permute-start = (bf16[64,40,768]{2,1,0:T(8,128)(2,1)}, bf16[64,40,768]{2,1,0:T(8,128)(2,1)}, u32[]{:S(2)}, u32[]{:S(2)}) collective-permute-start(bf16[64,40,768]{2,1,0:T(8,128)(2,1)} %all_to_all.21), channel_id=1, source_target_pairs={{0,8},{8,0},{1,9},{9,1},{2,10},{10,2},{3,11},{11,3},{4,12},{12,4},... | collective-permute-start | bytes 11796488 | tf_op jit(solution)/shard_map/ppermute | solution.py:112
  204.2 29.3 %all-to-all-start.2 = ((f32[16,40,768]{2,1,0:T(8,128)}), f32[16,40,768]{2,1,0:T(8,128)S(1)}, u32[]{:S(2)}, u32[]{:S(2)}) async-start(f32[16,40,768]{2,1,0:T(8,128)} %broadcast_in_dim.7), calls=%async_computation.2 | async-start | bytes 3932160 | tf_op jit(solution)/shard_map/all_to_all | solution.py:31
  239.8 1.4 copy-start.1
  239.8 1.9 copy-start.2
